TPU v7x, 256 devices: a whole 4x4x8 slice. The times are simulated.
256 devices in a mesh: ctx: 32 (over y, x, core), head: 8 (over z).
Axes of the slice: x: 4, y: 4, z: 8, core: 2. Of those that a mesh axis runs over, the one named last changes fastest.
Arguments:
- queries: bfloat16 [8192, 4096], P('ctx', 'head'), may hold values from -6 to 6
- key_rows: bfloat16 [8192, 4096], P('ctx', 'head'), may hold values from -6 to 6
- values: bfloat16 [8192, 4096], P('ctx', 'head'), may hold values from -6 to 6
- log_decay: float32 [8192, 32], P('ctx', 'head'), may hold values from 0 to 1, as said below
- head_gain: bfloat16 [4096], P('head'), may hold values from 0.099609375 to 1.8984375
- out_weight: bfloat16 [3072, 4096], P('ctx', 'head'), may hold values from -0.09375 to 0.09375
- residual: bfloat16 [8192, 3072], P('ctx', 'head'), may hold values from -6 to 6
- norm_gain: bfloat16 [3072], P('head'), may hold values from 0.099609375 to 1.8984375
- router: bfloat16 [3072, 32], replicated, may hold values from -0.21875 to 0.21875
- expert_ids: int32 [8192, 2], P('ctx'), may hold values from 0 to 31, all different within a row; in each aligned block of 256 rows (0 to 255, 256 to 511, ...) at most 24 rows name the same one
- gate_weight: bfloat16 [32, 3072, 5120], P('ctx', None, 'head'), may hold values from -0.109375 to 0.109375
- up_weight: bfloat16 [32, 3072, 5120], P('ctx', None, 'head'), may hold values from -0.109375 to 0.109375
- down_weight: bfloat16 [32, 5120, 3072], P('ctx', 'head'), may hold values from -0.125 to 0.125
Outputs:
- layer_out: float32 [8192, 3072], P('ctx', 'head')
Inputs may be any that keep to these rules, and one draw needn't show every extreme that they name: `log_decay`: amounts by which a head's state decays at a position: the state is multiplied by exp(-value). `expert_ids`: each row names 2 different experts; among the rows of one block of 256 positions no expert is named more than 24 times, a bound that some block reaches.
All inputs are finite; a program needn't handle non-finite values.
Results may differ from a plain program's by a relative error of at most 0.007.
Values may be sent and summed in bfloat16 or wider, within the bound.
No kernel may reach another device: no remote copies, remote signals or barrier semaphores. Data moves between devices by JAX's collectives and lax.ppermute only.
A program may use at most 128 MiB of HBM per device.

v0:
```python
import jax
import jax.numpy as jnp
from jax import lax
from jax.sharding import PartitionSpec as P

HEAD_DIM = 128
TOP = 2
HIGH = lax.Precision.HIGHEST
EPSILON = 1e-05


def combine(earlier, later):
    rows = HEAD_DIM
    decay_late = later[:, rows : rows + 1, 0:1]
    state = decay_late * earlier[:, :rows] + later[:, :rows]
    decay = earlier[:, rows : rows + 1] * later[:, rows : rows + 1]
    pad = jnp.zeros((later.shape[0], later.shape[1] - rows - 1, later.shape[2]), later.dtype)
    return jnp.concatenate([state, decay, pad], axis=1)


def exclusive_scan(packed, axis):
    count, mine = (lax.axis_size(axis), lax.axis_index(axis))
    rows = HEAD_DIM
    identity = jnp.zeros_like(packed).at[:, rows].set(1.0)
    window = packed
    before = identity
    shift = 1
    while shift < count:
        pairs = [(j, j + shift) for j in range(count - shift)]
        got = lax.ppermute(window, axis, pairs)
        got = jnp.where(mine >= shift, got, identity)
        before = combine(got, before)
        if 2 * shift < count:
            window = combine(got, window)
        shift *= 2
    return before[:, :rows]


def on_device(
    queries,
    key_rows,
    values,
    log_decay,
    head_gain,
    out_weight,
    residual,
    norm_gain,
    router,
    expert_ids,
    gate_weight,
    up_weight,
    down_weight,
):
    rows = queries.shape[0]
    heads_here = log_decay.shape[1]
    groups = lax.axis_size("head")
    query_heads = queries.reshape(rows, heads_here, HEAD_DIM)
    key_heads = key_rows.reshape(rows, heads_here, HEAD_DIM)
    value_heads = values.reshape(rows, heads_here, HEAD_DIM)
    cumulative = jnp.cumsum(log_decay, axis=0)
    scores = jnp.einsum("thd,jhd->htj", query_heads, key_heads, preferred_element_type=jnp.float32)
    causal = jnp.arange(rows)[:, None] >= jnp.arange(rows)[None, :]
    gap = cumulative.T[:, :, None] - cumulative.T[:, None, :]
    weight = jnp.where(causal[None], jnp.exp(-jnp.where(causal[None], gap, 0.0)), 0.0)
    weighted = (scores * weight).astype(jnp.bfloat16)
    inner = jnp.einsum("htj,jhd->thd", weighted, value_heads, preferred_element_type=jnp.float32)
    value_wide = value_heads.astype(jnp.float32)
    tail = jnp.exp(cumulative - cumulative[-1:])
    keys_tail = key_heads.astype(jnp.float32) * tail[:, :, None]
    local_state = jnp.einsum("jhd,jhe->hde", keys_tail, value_wide, precision=HIGH)
    shard_decay = jnp.exp(-cumulative[-1])
    decay_rows = jnp.broadcast_to(shard_decay[:, None, None], (heads_here, 1, HEAD_DIM))
    pad = jnp.zeros((heads_here, 7, HEAD_DIM), jnp.float32)
    packed = jnp.concatenate([local_state, decay_rows, pad], axis=1)
    incoming = exclusive_scan(packed, "ctx")
    query_decayed = query_heads.astype(jnp.float32) * jnp.exp(-cumulative)[:, :, None]
    outer = jnp.einsum("thd,hde->the", query_decayed, incoming, precision=HIGH)
    mixed = inner + outer
    mean_sq = jnp.mean(mixed * mixed, axis=-1, keepdims=True)
    gain_heads = head_gain.astype(jnp.float32).reshape(heads_here, HEAD_DIM)
    normed = (
        (mixed * lax.rsqrt(mean_sq + EPSILON) * gain_heads)
        .astype(jnp.bfloat16)
        .reshape(rows, heads_here * HEAD_DIM)
    )
    width = residual.shape[1]
    full = width * groups
    weight_all = lax.all_gather(out_weight, "ctx", axis=0, tiled=True).reshape(
        groups, width, heads_here * HEAD_DIM
    )
    partial_proj = jnp.einsum(
        "tk,gck->gtc", normed, weight_all, preferred_element_type=jnp.float32
    ).astype(jnp.bfloat16)
    total = lax.psum_scatter(partial_proj, "head", scatter_dimension=0, tiled=True)
    stream_mine = residual.astype(jnp.float32) + total[0].astype(jnp.float32)
    sq_part = jnp.sum(stream_mine * stream_mine, axis=1)
    sq_hi = sq_part.astype(jnp.bfloat16)
    sq_lo = (sq_part - sq_hi.astype(jnp.float32)).astype(jnp.bfloat16)
    experts = router.shape[1]
    capacity = 3 * rows * TOP // (2 * experts)
    lane = 128
    wide = width + lane
    other_id = expert_ids[:, ::-1].astype(jnp.bfloat16)
    token_rows = jnp.concatenate(
        [
            stream_mine.astype(jnp.bfloat16),
            sq_hi[:, None],
            sq_lo[:, None],
            jnp.zeros((rows, lane - 2), jnp.bfloat16),
        ],
        axis=1,
    )
    token_rows = jnp.concatenate([token_rows, jnp.zeros((8, wide), jnp.bfloat16)], axis=0)
    flat_ids = expert_ids.reshape(-1)
    onehot = (flat_ids[:, None] == jnp.arange(experts, dtype=jnp.int32)[None, :]).astype(jnp.int32)
    before = jnp.cumsum(onehot, axis=0) - onehot
    position = jnp.sum(before * onehot, axis=1)
    slot = flat_ids * capacity + position
    owner = jnp.arange(rows * TOP, dtype=jnp.int32) // TOP
    slot_token = jnp.full((experts * capacity,), rows, jnp.int32).at[slot].set(owner)
    slot_other = jnp.zeros((experts * capacity,), jnp.bfloat16).at[slot].set(other_id.reshape(-1))
    outgoing = token_rows[slot_token]
    outgoing = outgoing.at[:, width + 2].set(slot_other).reshape(experts, capacity, wide)
    arriving = lax.all_to_all(outgoing, "ctx", split_axis=0, concat_axis=0, tiled=True)
    flat = arriving.reshape(-1, wide)
    slots_here = flat.shape[0]
    sq_rows = jnp.transpose(flat[:, width : width + 2]).reshape(2 * slots_here // width, width)
    spare = 7 - sq_rows.shape[0]
    extra = jnp.concatenate(
        [norm_gain[None, :], sq_rows, jnp.zeros((spare, width), jnp.bfloat16)], axis=0
    )
    gathered = lax.all_gather(jnp.concatenate([flat[:, :width], extra], axis=0), "head", axis=0)
    stream_blocks = gathered[:, :slots_here].astype(jnp.float32)
    gain_blocks = gathered[:, slots_here].astype(jnp.float32)
    sq_parts = gathered[:, slots_here + 1 : slots_here + 1 + sq_rows.shape[0]].astype(jnp.float32)
    sq_parts = sq_parts.reshape(groups, 2, slots_here)
    stream_sq = jnp.sum(sq_parts, axis=(0, 1))[None, :, None] / full
    other_here = flat[:, width + 2].astype(jnp.int32)
    moe_in = (stream_blocks * lax.rsqrt(stream_sq + EPSILON) * gain_blocks[:, None, :]).astype(
        jnp.bfloat16
    )
    router_blocks = router.reshape(groups, width, router.shape[1])
    logits = jnp.einsum("grc,gce->re", moe_in, router_blocks, preferred_element_type=jnp.float32)
    expert_here = lax.axis_index("ctx")
    names = jnp.arange(experts, dtype=jnp.int32)[None, :]
    own_logit = jnp.sum(jnp.where(names == expert_here, logits, 0.0), axis=1)
    other_logit = jnp.sum(jnp.where(names == other_here[:, None], logits, 0.0), axis=1)
    mix_here = jax.nn.sigmoid(own_logit - other_logit)
    mix_hi = mix_here.astype(jnp.bfloat16)
    mix_lo = (mix_here - mix_hi.astype(jnp.float32)).astype(jnp.bfloat16)
    hidden = gate_weight.shape[2]
    gate = jnp.einsum(
        "grc,gcf->rf",
        moe_in,
        gate_weight[0].reshape(groups, width, hidden),
        preferred_element_type=jnp.float32,
    )
    up = jnp.einsum(
        "grc,gcf->rf",
        moe_in,
        up_weight[0].reshape(groups, width, hidden),
        preferred_element_type=jnp.float32,
    )
    activated = (jax.nn.silu(gate) * up).astype(jnp.bfloat16)
    down = down_weight[0].reshape(down_weight.shape[1], groups, width)
    partial_value = jnp.einsum(
        "rf,fgc->grc", activated, down, preferred_element_type=jnp.float32
    ).astype(jnp.bfloat16)
    summed = lax.psum_scatter(partial_value, "head", scatter_dimension=0, tiled=True)[0]
    back = jnp.concatenate(
        [summed, mix_hi[:, None], mix_lo[:, None], jnp.zeros((slots_here, lane - 2), jnp.bfloat16)],
        axis=1,
    ).reshape(arriving.shape[0], arriving.shape[1], wide)
    returned = lax.all_to_all(back, "ctx", split_axis=0, concat_axis=0, tiled=True)
    picked_rows = returned.reshape(experts * capacity, wide)[slot].astype(jnp.float32)
    picked_rows = picked_rows.reshape(rows, TOP, wide)
    mix_weights = picked_rows[:, :, width] + picked_rows[:, :, width + 1]
    moe_out = jnp.sum(picked_rows[:, :, :width] * mix_weights[:, :, None], axis=1)
    return stream_mine + moe_out


def solution(mesh):
    placed = (
        P("ctx", "head"),
        P("ctx", "head"),
        P("ctx", "head"),
        P("ctx", "head"),
        P("head"),
        P("ctx", "head"),
        P("ctx", "head"),
        P("head"),
        P(),
        P("ctx", None),
        P("ctx", None, "head"),
        P("ctx", None, "head"),
        P("ctx", "head", None),
    )
    return jax.shard_map(
        on_device, mesh=mesh, in_specs=placed, out_specs=P("ctx", "head"), check_vma=False
    )
```

profile of v0, /device:TPU:1, one launch (start us, length us, event | category | flops | bytes accessed | tf_op | source)
XLA Modules:
  0.0 318.7 jit_solution(5503128526121776230)
XLA Ops:
  11.9 4.5 %collective-permute-start = (f32[4,136,128]{2,1,0:T(8,128)S(1)}, f32[4,136,128]{2,1,0:T(8,128)S(1)}, u32[]{:S(2)}, u32[]{:S(2)}) collective-permute-start(f32[4,136,128]{2,1,0:T(8,128)S(1)} %maximum_maximum_fusion.2), channel_id=1, source_target_pairs={{0,8},{8,16},{16,24},{24,32},{32,40},{40,48},{48,56},{56,64},{64,7... | collective-permute-start | bytes 835592 | tf_op jit(solution)/shard_map/ppermute | solution.py:30
  16.5 3.4 %collective-permute-done = f32[4,136,128]{2,1,0:T(8,128)S(1)} collective-permute-done((f32[4,136,128]{2,1,0:T(8,128)S(1)}, f32[4,136,128]{2,1,0:T(8,128)S(1)}, u32[]{:S(2)}, u32[]{:S(2)}) %collective-permute-start) | collective-permute-done | bytes 278560 | tf_op jit(solution)/shard_map/ppermute | solution.py:30
  23.5 4.4 %collective-permute-done.1 = f32[4,136,128]{2,1,0:T(8,128)S(1)} collective-permute-done((f32[4,136,128]{2,1,0:T(8,128)S(1)}, f32[4,136,128]{2,1,0:T(8,128)S(1)}, u32[]{:S(2)}, u32[]{:S(2)}) %collective-permute-start.1) | collective-permute-done | bytes 278560 | tf_op jit(solution)/shard_map/ppermute | solution.py:30
  28.2 5.1 %collective-permute-start.2 = (f32[4,136,128]{2,1,0:T(8,128)S(1)}, f32[4,136,128]{2,1,0:T(8,128)S(1)}, u32[]{:S(2)}, u32[]{:S(2)}) collective-permute-start(f32[4,136,128]{2,1,0:T(8,128)S(1)} %maximum_maximum_fusion.4), channel_id=1, source_target_pairs={{0,32},{8,40},{16,48},{24,56},{32,64},{40,72},{48,80},{56,88},{64,... | collective-permute-start | bytes 835592 | tf_op jit(solution)/shard_map/ppermute | solution.py:30
  34.0 3.2 %collective-permute-done.2 = f32[4,136,128]{2,1,0:T(8,128)S(1)} collective-permute-done((f32[4,136,128]{2,1,0:T(8,128)S(1)}, f32[4,136,128]{2,1,0:T(8,128)S(1)}, u32[]{:S(2)}, u32[]{:S(2)}) %collective-permute-start.2) | collective-permute-done | bytes 278560 | tf_op jit(solution)/shard_map/ppermute | solution.py:30
  37.5 5.9 %collective-permute-start.3 = (f32[4,136,128]{2,1,0:T(8,128)S(1)}, f32[4,136,128]{2,1,0:T(8,128)S(1)}, u32[]{:S(2)}, u32[]{:S(2)}) collective-permute-start(f32[4,136,128]{2,1,0:T(8,128)S(1)} %maximum_maximum_fusion.5), channel_id=1, source_target_pairs={{0,64},{8,72},{16,80},{24,88},{32,96},{40,104},{48,112},{56,120},{... | collective-permute-start | bytes 835592 | tf_op jit(solution)/shard_map/ppermute | solution.py:30
  43.6 3.9 %collective-permute-done.3 = f32[4,136,128]{2,1,0:T(8,128)S(1)} collective-permute-done((f32[4,136,128]{2,1,0:T(8,128)S(1)}, f32[4,136,128]{2,1,0:T(8,128)S(1)}, u32[]{:S(2)}, u32[]{:S(2)}) %collective-permute-start.3) | collective-permute-done | bytes 278560 | tf_op jit(solution)/shard_map/ppermute | solution.py:30
  47.7 5.4 %collective-permute-start.4 = (f32[4,136,128]{2,1,0:T(8,128)S(1)}, f32[4,136,128]{2,1,0:T(8,128)S(1)}, u32[]{:S(2)}, u32[]{:S(2)}) collective-permute-start(f32[4,136,128]{2,1,0:T(8,128)S(1)} %maximum_maximum_fusion.6), channel_id=1, source_target_pairs={{0,128},{8,136},{16,144},{24,152},{32,160},{40,168},{48,176},{56,1... | collective-permute-start | bytes 835592 | tf_op jit(solution)/shard_map/ppermute | solution.py:30
  57.6 15.2 %all-gather.4.cloned.1.call-done = bf16[3072,512]{1,0:T(8,128)(2,1)} async-done(((bf16[96,512]{1,0:T(8,128)(2,1)}), bf16[3072,512]{1,0:T(8,128)(2,1)}) %all-gather.4.cloned.1.call-update) | async-done | bytes 3145744 | tf_op jit(solution)/shard_map/all_gather | solution.py:88
  72.8 4.1 %fusion.8 = bf16[8,256,384]{2,1,0:T(8,128)(2,1)} fusion(bf16[256,512,1]{0,1,2:T(8,128)(2,1)S(1)} %bitcast.154, bf16[8,384,512]{2,1,0:T(8,128)(2,1)} %bitcast.153), kind=kOutput, calls=%fused_computation.16 | convolution fusion | flops 806092800 | bytes 4980736 | tf_op jit(solution)/shard_map/tk,gck->gtc/dot_general | solution.py:91
  79.7 3.8 %scatter_custom_fusion.1 = bf16[768]{0:T(1024)(128)(2,1)S(1)} fusion(s32[512]{0:T(512)S(1)} %bitcast.165, bf16[512]{0:T(512)(128)(2,1)S(1)} %reshape.350, bf16[]{:T(256)} %constant.126.clone.1), kind=kCustom, calls=%fused_computation.150 | custom fusion | bytes 1538 | tf_op jit(solution)/shard_map/scatter | solution.py:121
  86.5 27.3 %reduce-scatter.3.cloned.1.call-done = bf16[1,256,384]{2,1,0:T(8,128)(2,1)} async-done(((bf16[8,256,384]{2,1,0:T(8,128)(2,1)}), bf16[1,256,384]{2,1,0:T(8,128)(2,1)}) %reduce-scatter.3.cloned.1.call-update) | async-done | bytes 196624 | tf_op jit(solution)/shard_map/reduce_scatter | solution.py:94
  115.4 3.3 %gather_fusion = bf16[768,512]{1,0:T(8,128)(2,1)} fusion(bf16[264,512]{1,0:T(8,128)(2,1)S(1)} %concatenate.40, s32[1024]{0:T(1024)S(1)} %pad_clamp_fusion.1), kind=kCustom, calls=%fused_computation | custom fusion | bytes 1575936 | tf_op jit(solution)/shard_map/gather | solution.py:122
  122.8 11.6 %all-to-all-start = ((bf16[32,24,512]{2,1,0:T(8,128)(2,1)}), bf16[32,24,512]{2,1,0:T(8,128)(2,1)S(1)}, u32[]{:S(2)}, u32[]{:S(2)}) async-start(bf16[32,24,512]{2,1,0:T(8,128)(2,1)} %bitcast.15), calls=%async_computation.1 | async-start | bytes 1572864 | tf_op jit(solution)/shard_map/all_to_all | solution.py:124
  134.6 14.1 %all-to-all-done = bf16[32,24,512]{2,1,0:T(8,128)(2,1)S(1)} async-done(((bf16[32,24,512]{2,1,0:T(8,128)(2,1)}), bf16[32,24,512]{2,1,0:T(8,128)(2,1)S(1)}, u32[]{:S(2)}, u32[]{:S(2)}) %all-to-all-start) | async-done | bytes 786464 | tf_op jit(solution)/shard_map/all_to_all | solution.py:124
  150.0 5.0 %copy.212 = bf16[80,8,8,384]{3,2,1,0:T(8,128)(2,1)} copy(bf16[80,8,8,384]{3,1,2,0:T(8,128)(2,1)} %bitcast.151) | data formatting | bytes 7864320
  155.0 50.2 %all-gather.6.cloned.1.call-done = bf16[6208,384]{1,0:T(8,128)(2,1)} async-done(((bf16[776,384]{1,0:T(8,128)(2,1)}), bf16[6208,384]{1,0:T(8,128)(2,1)}) %all-gather.6.cloned.1.call-update) | async-done | bytes 4767760 | tf_op jit(solution)/shard_map/all_gather | solution.py:132
  206.9 7.2 %fusion.76 = f32[768,640,1]{1,0,2:T(8,128)S(1)} fusion(bf16[8,384,640]{2,1,0:T(8,128)(2,1)} %bitcast.176, bf16[8,776,384]{2,1,0:T(8,128)(2,1)} %bitcast.173, f32[8,384]{1,0:T(8,128)S(1)} %bitcast.158, f32[768]{0:T(1024)S(1)} %add_rsqrt_fusion), kind=kOutput, calls=%fused_computation.159 | convolution fusion | flops 3029336064 | bytes 10632192 | tf_op jit(solution)/shard_map/grc,gcf->rf/dot_general | solution.py:152
  214.2 4.0 %fusion.9 = bf16[768,640,1]{1,0,2:T(8,128)(2,1)S(1)} fusion(bf16[8,384,640]{2,1,0:T(8,128)(2,1)S(1)} %bitcast.177, f32[768,640,1]{1,0,2:T(8,128)S(1)} %fusion.76, bf16[8,776,384]{2,1,0:T(8,128)(2,1)S(1)} %bitcast.175, f32[8,384]{1,0:T(8,128)S(1)} %bitcast.159, f32[768]{0:T(1024)S(1)} %add_rsqrt_fusion), kind=kOutput, calls=%fused_computation.18 | convolution fusion | flops 3032285184 | bytes 11616256 | tf_op jit(solution)/shard_map/grc,gcf->rf/dot_general | solution.py:158
  218.2 5.6 %convert_bitcast_fusion = bf16[8,768,384]{2,1,0:T(8,128)(2,1)} fusion(bf16[768,640,1]{1,0,2:T(8,128)(2,1)S(1)} %fusion.9, bf16[640,8,384]{2,1,0:T(8,128)(2,1)S(1)} %bitcast.152), kind=kOutput, calls=%fused_computation.5 | convolution fusion | flops 3022258176 | bytes 9633792 | tf_op jit(solution)/shard_map/rf,fgc->grc/dot_general | solution.py:166
  224.7 4.0 %select_reduce_fusion = (f32[768]{0:T(1024)S(1)}, f32[768]{0:T(1024)S(1)}) fusion(s32[768]{0:T(1024)S(1)} %convert_reduce_fusion, pred[32]{0:T(512)(128)(4,1)S(1)} %iota_compare_fusion.4, bf16[4,8,8,384]{3,2,1,0:T(8,128)(2,1)S(1)} %bitcast.178, bf16[8,776,384]{2,1,0:T(8,128)(2,1)} %bitcast.174, f32[8,384]{1,0:T(8,128)S(1)} %bitcast.160, ...), kind=kOutput, calls=%fused_computation.97 | convolution fusion | flops 160553472 | bytes 4939808 | tf_op jit(solution)/shard_map/grc,gce->re/dot_general | solution.py:143
  229.4 53.5 %reduce-scatter.5.cloned.1.call-done = bf16[1,768,384]{2,1,0:T(8,128)(2,1)} async-done(((bf16[8,768,384]{2,1,0:T(8,128)(2,1)}), bf16[1,768,384]{2,1,0:T(8,128)(2,1)}) %reduce-scatter.5.cloned.1.call-update) | async-done | bytes 589840 | tf_op jit(solution)/shard_map/reduce_scatter | solution.py:169
  285.1 7.6 %all-to-all-start.1 = ((bf16[32,24,512]{2,1,0:T(8,128)(2,1)}), bf16[32,24,512]{2,1,0:T(8,128)(2,1)S(1)}, u32[]{:S(2)}, u32[]{:S(2)}) async-start(bf16[32,24,512]{2,1,0:T(8,128)(2,1)} %maximum_maximum_fusion), calls=%async_computation.3 | async-start | bytes 1572864 | tf_op jit(solution)/shard_map/all_to_all | solution.py:174
  292.8 14.2 %all-to-all-done.1 = bf16[32,24,512]{2,1,0:T(8,128)(2,1)S(1)} async-done(((bf16[32,24,512]{2,1,0:T(8,128)(2,1)}), bf16[32,24,512]{2,1,0:T(8,128)(2,1)S(1)}, u32[]{:S(2)}, u32[]{:S(2)}) %all-to-all-start.1) | async-done | bytes 786464 | tf_op jit(solution)/shard_map/all_to_all | solution.py:174
  (146 shorter events, 38.4 us)
Async XLA Ops:
  6.5 26.8 %copy-start = (bf16[256,512]{1,0:T(8,128)(2,1)S(1)}, bf16[256,512]{1,0:T(8,128)(2,1)}, u32[]{:S(2)}) copy-start(bf16[256,512]{1,0:T(8,128)(2,1)} %param.17) | copy-start | bytes 786436
  6.5 21.4 %copy-start.1 = (f32[4,136,128]{2,1,0:T(8,128)S(1)}, f32[4,136,128]{2,1,0:T(8,128)}, u32[]{:S(2)}) copy-start(f32[4,136,128]{2,1,0:T(8,128)} %constant.121.clone.1) | copy-start | bytes 835588
  6.5 26.8 %copy-start.5 = (bf16[256,512]{1,0:T(8,128)(2,1)S(1)}, bf16[256,512]{1,0:T(8,128)(2,1)}, u32[]{:S(2)}) copy-start(bf16[256,512]{1,0:T(8,128)(2,1)} %param.19) | copy-start | bytes 786436
  6.5 66.2 %all-gather.4.cloned.1.call-start = ((), (), s32[]{:S(2)}) async-start(), calls=%async_computation.4 | async-start | bytes 3244032 | tf_op jit(solution)/shard_map/all_gather | solution.py:88
  11.9 8.0 %collective-permute-start = (f32[4,136,128]{2,1,0:T(8,128)S(1)}, f32[4,136,128]{2,1,0:T(8,128)S(1)}, u32[]{:S(2)}, u32[]{:S(2)}) collective-permute-start(f32[4,136,128]{2,1,0:T(8,128)S(1)} %maximum_maximum_fusion.2), channel_id=1, source_target_pairs={{0,8},{8,16},{16,24},{24,32},{32,40},{40,48},{48,56},{56,64},{64,7... | collective-permute-start | bytes 835592 | tf_op jit(solution)/shard_map/ppermute | solution.py:30
  16.4 97.5 %reduce-scatter.3.cloned.1.call-start = ((), (), s32[]{:S(2)}) async-start(), calls=%async_computation.5 | async-start | bytes 1769472 | tf_op jit(solution)/shard_map/reduce_scatter | solution.py:94
  20.2 23.3 %copy-start.7 = (bf16[512]{0:T(512)(128)(2,1)S(1)}, bf16[512]{0:T(512)(128)(2,1)}, u32[]{:S(2)}) copy-start(bf16[512]{0:T(512)(128)(2,1)} %param.21) | copy-start | bytes 3076
  20.2 7.7 %collective-permute-start.1 = (f32[4,136,128]{2,1,0:T(8,128)S(1)}, f32[4,136,128]{2,1,0:T(8,128)S(1)}, u32[]{:S(2)}, u32[]{:S(2)}) collective-permute-start(f32[4,136,128]{2,1,0:T(8,128)S(1)} %maximum_maximum_fusion.3), channel_id=1, source_target_pairs={{0,16},{8,24},{16,32},{24,40},{32,48},{40,56},{48,64},{56,72},{64,... | collective-permute-start | bytes 835592 | tf_op jit(solution)/shard_map/ppermute | solution.py:30
  28.2 9.1 %collective-permute-start.2 = (f32[4,136,128]{2,1,0:T(8,128)S(1)}, f32[4,136,128]{2,1,0:T(8,128)S(1)}, u32[]{:S(2)}, u32[]{:S(2)}) collective-permute-start(f32[4,136,128]{2,1,0:T(8,128)S(1)} %maximum_maximum_fusion.4), channel_id=1, source_target_pairs={{0,32},{8,40},{16,48},{24,56},{32,64},{40,72},{48,80},{56,88},{64,... | collective-permute-start | bytes 835592 | tf_op jit(solution)/shard_map/ppermute | solution.py:30
  37.5 9.9 %collective-permute-start.3 = (f32[4,136,128]{2,1,0:T(8,128)S(1)}, f32[4,136,128]{2,1,0:T(8,128)S(1)}, u32[]{:S(2)}, u32[]{:S(2)}) collective-permute-start(f32[4,136,128]{2,1,0:T(8,128)S(1)} %maximum_maximum_fusion.5), channel_id=1, source_target_pairs={{0,64},{8,72},{16,80},{24,88},{32,96},{40,104},{48,112},{56,120},{... | collective-permute-start | bytes 835592 | tf_op jit(solution)/shard_map/ppermute | solution.py:30
  47.7 8.9 %collective-permute-start.4 = (f32[4,136,128]{2,1,0:T(8,128)S(1)}, f32[4,136,128]{2,1,0:T(8,128)S(1)}, u32[]{:S(2)}, u32[]{:S(2)}) collective-permute-start(f32[4,136,128]{2,1,0:T(8,128)S(1)} %maximum_maximum_fusion.6), channel_id=1, source_target_pairs={{0,128},{8,136},{16,144},{24,152},{32,160},{40,168},{48,176},{56,1... | collective-permute-start | bytes 835592 | tf_op jit(solution)/shard_map/ppermute | solution.py:30
  57.4 19.4 %copy-start.6 = (s32[256,2]{0,1:T(2,128)S(1)}, s32[256,2]{0,1:T(2,128)}, u32[]{:S(2)}) copy-start(s32[256,2]{0,1:T(2,128)} %param.26) | copy-start | bytes 6148
  57.6 56.3 %copy-start.3 = (bf16[256,384]{1,0:T(8,128)(2,1)S(1)}, bf16[256,384]{1,0:T(8,128)(2,1)}, u32[]{:S(2)}) copy-start(bf16[256,384]{1,0:T(8,128)(2,1)} %param.23) | copy-start | bytes 589828
  115.4 19.0 %copy-start.8 = (bf16[384]{0:T(512)(128)(2,1)S(1)}, bf16[384]{0:T(512)(128)(2,1)}, u32[]{:S(2)}) copy-start(bf16[384]{0:T(512)(128)(2,1)} %param.24) | copy-start | bytes 2308
  122.8 25.9 %all-to-all-start = ((bf16[32,24,512]{2,1,0:T(8,128)(2,1)}), bf16[32,24,512]{2,1,0:T(8,128)(2,1)S(1)}, u32[]{:S(2)}, u32[]{:S(2)}) async-start(bf16[32,24,512]{2,1,0:T(8,128)(2,1)} %bitcast.15), calls=%async_computation.1 | async-start | bytes 1572864 | tf_op jit(solution)/shard_map/all_to_all | solution.py:124
  134.4 70.8 %all-gather.6.cloned.1.call-start = ((), (), s32[]{:S(2)}) async-start(), calls=%async_computation.7 | async-start | bytes 5363712 | tf_op jit(solution)/shard_map/all_gather | solution.py:132
  150.0 133.0 %reduce-scatter.5.cloned.1.call-start = ((), (), s32[]{:S(2)}) async-start(), calls=%async_computation.6 | async-start | bytes 5308416 | tf_op jit(solution)/shard_map/reduce_scatter | solution.py:169
  206.9 7.3 %copy-start.9 = (bf16[6208,384]{1,0:T(8,128)(2,1)S(1)}, bf16[6208,384]{1,0:T(8,128)(2,1)}, u32[]{:S(2)}) copy-start(bf16[6208,384]{1,0:T(8,128)(2,1)} %all-gather.6.cloned.1.call-done) | copy-start | bytes 14303236
  206.9 7.3 %copy-start.10 = (bf16[1,3072,640]{2,1,0:T(8,128)(2,1)S(1)}, bf16[1,3072,640]{2,1,0:T(8,128)(2,1)}, u32[]{:S(2)}) copy-start(bf16[1,3072,640]{2,1,0:T(8,128)(2,1)} %param.28) | copy-start | bytes 11796484
  214.1 4.0 %copy-start.2 = (bf16[80,8,8,384]{3,2,1,0:T(8,128)(2,1)S(1)}, bf16[80,8,8,384]{3,2,1,0:T(8,128)(2,1)}, u32[]{:S(2)}) copy-start(bf16[80,8,8,384]{3,2,1,0:T(8,128)(2,1)} %copy.212) | copy-start | bytes 11796484
  223.8 0.9 copy-start.11
  285.1 21.8 %all-to-all-start.1 = ((bf16[32,24,512]{2,1,0:T(8,128)(2,1)}), bf16[32,24,512]{2,1,0:T(8,128)(2,1)S(1)}, u32[]{:S(2)}, u32[]{:S(2)}) async-start(bf16[32,24,512]{2,1,0:T(8,128)(2,1)} %maximum_maximum_fusion), calls=%async_computation.3 | async-start | bytes 1572864 | tf_op jit(solution)/shard_map/all_to_all | solution.py:174
  307.0 4.4 %copy-start.4 = (bf16[1,256,384]{2,1,0:T(8,128)(2,1)S(1)}, bf16[1,256,384]{2,1,0:T(8,128)(2,1)}, u32[]{:S(2)}) copy-start(bf16[1,256,384]{2,1,0:T(8,128)(2,1)} %reduce-scatter.3.cloned.1.call-done) | copy-start | bytes 589828
Sparse Core Ops, SparseCore 0:
  16.5 56.1 all-gather.3
  77.0 36.8 reduce-scatter.2
  150.1 55.0 all-gather.5
  224.0 58.9 reduce-scatter.4
where the time goes:
time: 320 us; the launch traced here: 319 us
  waiting for transfers between devices  193 us (60%)
  starting transfers between devices  43.4 us (14%)
  matrix products  27.7 us (9%)
  local copies, waits for them, and re-layouts  26.6 us (8%)
  other arithmetic  14.7 us (5%)
  between operations  13.8 us (4%)
    reduce_scatter x1, waiting for transfers between devices, on_device(): lax.psum_scatter(partial_value, 'head', scatter_dimension=0, tiled=True)[0]  53.5 us
    all_gather x1, waiting for transfers between devices, on_device(): lax.all_gather(jnp.concatenate([flat[:, :width], extra], axis=0), 'head',...  50.2 us
    reduce_scatter x1, waiting for transfers between devices, on_device(): lax.psum_scatter(partial_proj, 'head', scatter_dimension=0, tiled=True)  27.3 us
    ppermute x5, starting transfers between devices, exclusive_scan(): got = lax.ppermute(window, axis, pairs)  24.1 us
    ppermute x5, waiting for transfers between devices, exclusive_scan(): got = lax.ppermute(window, axis, pairs)  18 us
    all_gather x1, waiting for transfers between devices, on_device(): lax.all_gather(out_weight, 'ctx', axis=0, tiled=True)  15.2 us
    all_to_all x1, waiting for transfers between devices, on_device(): lax.all_to_all(back, 'ctx', split_axis=0, concat_axis=0, tiled=True)  14.2 us
    all_to_all x1, waiting for transfers between devices, on_device(): lax.all_to_all(outgoing, 'ctx', split_axis=0, concat_axis=0, tiled=True)  14.1 us
  transfers between devices with their start and end apart: 11, of which 11 were waited for; matrix products, arithmetic and copies ran while one was open for 7% of the time, Pallas kernels for 0%

commit v1 on v0

--- a/solution.py
+++ b/solution.py
@@ -85,9 +85,9 @@
     )
     width = residual.shape[1]
     full = width * groups
-    weight_all = lax.all_gather(out_weight, "ctx", axis=0, tiled=True).reshape(
-        groups, width, heads_here * HEAD_DIM
-    )
+    weight_all = jnp.concatenate(
+        lax.all_to_all(jnp.stack([out_weight] * lax.axis_size("ctx")), "ctx", 0, 0), axis=0
+    ).reshape(groups, width, heads_here * HEAD_DIM)
     partial_proj = jnp.einsum(
         "tk,gck->gtc", normed, weight_all, preferred_element_type=jnp.float32
     ).astype(jnp.bfloat16)

time: 320 us -> 356 us (1.11)
  starting transfers between devices: 43.4 us -> 55.4 us
  waiting for transfers between devices: 193 us -> 203 us
  other arithmetic: 14.7 us -> 23.2 us
  local copies, waits for them, and re-layouts: 26.6 us -> 30.8 us
    ppermute x5, waiting for transfers between devices: 18 us -> 40.3 us  [exclusive_scan(): got = lax.ppermute(window, axis, pairs)]
    all_gather x1 -> x0, waiting for transfers between devices: 15.2 us -> none  [on_device(): lax.all_gather(out_weight, 'ctx', axis=0, tiled=True)]
    all_to_all x0 -> x1, starting transfers between devices: none -> 9.59 us  [on_device(): lax.all_to_all(jnp.stack([out_weight] * lax.axis_size('ctx')), 'ctx', 0, 0)]
    unnamed x30 -> x46, local copies, waits for them, and re-layouts: 6.05 us -> 8.05 us
  transfers between devices with their start and end apart: 11 -> 11, of which waited for: 11 -> 9; matrix products, arithmetic and copies ran while one was open for 7% -> 10% of each run, Pallas kernels for 0% -> 0%
where the time goes in v1:
time: 356 us; the launch traced here: 354 us
  waiting for transfers between devices  203 us (57%)
  starting transfers between devices  55.4 us (16%)
  local copies, waits for them, and re-layouts  30.8 us (9%)
  matrix products  28.6 us (8%)
  other arithmetic  23.2 us (7%)
  between operations  13.8 us (4%)
    reduce_scatter x1, waiting for transfers between devices, on_device(): lax.psum_scatter(partial_value, 'head', scatter_dimension=0, tiled=True)[0]  53.6 us
    all_gather x1, waiting for transfers between devices, on_device(): lax.all_gather(jnp.concatenate([flat[:, :width], extra], axis=0), 'head',...  50 us
    ppermute x5, waiting for transfers between devices, exclusive_scan(): got = lax.ppermute(window, axis, pairs)  40.3 us
    reduce_scatter x1, waiting for transfers between devices, on_device(): lax.psum_scatter(partial_proj, 'head', scatter_dimension=0, tiled=True)  30.4 us
    ppermute x5, starting transfers between devices, exclusive_scan(): got = lax.ppermute(window, axis, pairs)  26.7 us
    all_to_all x1, waiting for transfers between devices, on_device(): lax.all_to_all(back, 'ctx', split_axis=0, concat_axis=0, tiled=True)  14.2 us
    all_to_all x1, waiting for transfers between devices, on_device(): lax.all_to_all(outgoing, 'ctx', split_axis=0, concat_axis=0, tiled=True)  14.1 us
    all_to_all x1, starting transfers between devices, on_device(): lax.all_to_all(outgoing, 'ctx', split_axis=0, concat_axis=0, tiled=True)  11.4 us
  transfers between devices with their start and end apart: 11, of which 9 were waited for; matrix products, arithmetic and copies ran while one was open for 10% of the time, Pallas kernels for 0%

profile of v1, /device:TPU:1, one launch (start us, length us, event | category | flops | bytes accessed | tf_op | source)
XLA Modules:
  0.0 354.3 jit_solution(10889802590736705923)
XLA Ops:
  11.9 4.5 %collective-permute-start = (f32[4,136,128]{2,1,0:T(8,128)S(1)}, f32[4,136,128]{2,1,0:T(8,128)S(1)}, u32[]{:S(2)}, u32[]{:S(2)}) collective-permute-start(f32[4,136,128]{2,1,0:T(8,128)S(1)} %maximum_maximum_fusion.2), channel_id=1, source_target_pairs={{0,8},{8,16},{16,24},{24,32},{32,40},{40,48},{48,56},{56,64},{64,7... | collective-permute-start | bytes 835592 | tf_op jit(solution)/shard_map/ppermute | solution.py:30
  16.4 3.5 collective-permute-done
  22.2 3.8 %collective-permute-start.1 = (f32[4,136,128]{2,1,0:T(8,128)}, f32[4,136,128]{2,1,0:T(8,128)}, u32[]{:S(2)}, u32[]{:S(2)}) collective-permute-start(f32[4,136,128]{2,1,0:T(8,128)} %maximum_maximum_fusion.3), channel_id=1, source_target_pairs={{0,16},{8,24},{16,32},{24,40},{32,48},{40,56},{48,64},{56,72},{64,... | collective-permute-start | bytes 835592 | tf_op jit(solution)/shard_map/ppermute | solution.py:30
  28.0 9.6 %all-to-all-start = ((bf16[32,96,512]{2,1,0:T(8,128)(2,1)}), bf16[32,96,512]{2,1,0:T(8,128)(2,1)S(1)}, u32[]{:S(2)}, u32[]{:S(2)}) async-start(bf16[32,96,512]{2,1,0:T(8,128)(2,1)} %stack.2), calls=%async_computation | async-start | bytes 6291456 | tf_op jit(solution)/shard_map/all_to_all | solution.py:89
  42.2 5.5 %collective-permute-start.2 = (f32[4,136,128]{2,1,0:T(8,128)}, f32[4,136,128]{2,1,0:T(8,128)}, u32[]{:S(2)}, u32[]{:S(2)}) collective-permute-start(f32[4,136,128]{2,1,0:T(8,128)} %maximum_maximum_fusion.4), channel_id=1, source_target_pairs={{0,32},{8,40},{16,48},{24,56},{32,64},{40,72},{48,80},{56,88},{64,... | collective-permute-start | bytes 835592 | tf_op jit(solution)/shard_map/ppermute | solution.py:30
  50.3 28.2 %collective-permute-done.2 = f32[4,136,128]{2,1,0:T(8,128)} collective-permute-done((f32[4,136,128]{2,1,0:T(8,128)}, f32[4,136,128]{2,1,0:T(8,128)}, u32[]{:S(2)}, u32[]{:S(2)}) %collective-permute-start.2) | collective-permute-done | bytes 278560 | tf_op jit(solution)/shard_map/ppermute | solution.py:30
  81.3 7.7 %collective-permute-start.3 = (f32[4,136,128]{2,1,0:T(8,128)S(1)}, f32[4,136,128]{2,1,0:T(8,128)S(1)}, u32[]{:S(2)}, u32[]{:S(2)}) collective-permute-start(f32[4,136,128]{2,1,0:T(8,128)S(1)} %maximum_maximum_fusion.5), channel_id=1, source_target_pairs={{0,64},{8,72},{16,80},{24,88},{32,96},{40,104},{48,112},{56,120},{... | collective-permute-start | bytes 835592 | tf_op jit(solution)/shard_map/ppermute | solution.py:30
  89.1 4.9 %collective-permute-done.3 = f32[4,136,128]{2,1,0:T(8,128)S(1)} collective-permute-done((f32[4,136,128]{2,1,0:T(8,128)S(1)}, f32[4,136,128]{2,1,0:T(8,128)S(1)}, u32[]{:S(2)}, u32[]{:S(2)}) %collective-permute-start.3) | collective-permute-done | bytes 278560 | tf_op jit(solution)/shard_map/ppermute | solution.py:30
  95.2 5.2 %collective-permute-start.4 = (f32[4,136,128]{2,1,0:T(8,128)S(1)}, f32[4,136,128]{2,1,0:T(8,128)S(1)}, u32[]{:S(2)}, u32[]{:S(2)}) collective-permute-start(f32[4,136,128]{2,1,0:T(8,128)S(1)} %maximum_maximum_fusion.6), channel_id=1, source_target_pairs={{0,128},{8,136},{16,144},{24,152},{32,160},{40,168},{48,176},{56,1... | collective-permute-start | bytes 835592 | tf_op jit(solution)/shard_map/ppermute | solution.py:30
  100.8 3.8 %collective-permute-done.4 = f32[4,136,128]{2,1,0:T(8,128)S(1)} collective-permute-done((f32[4,136,128]{2,1,0:T(8,128)S(1)}, f32[4,136,128]{2,1,0:T(8,128)S(1)}, u32[]{:S(2)}, u32[]{:S(2)}) %collective-permute-start.4) | collective-permute-done | bytes 278560 | tf_op jit(solution)/shard_map/ppermute | solution.py:30
  112.3 3.8 %scatter_custom_fusion.1 = bf16[768]{0:T(1024)(128)(2,1)S(1)} fusion(s32[512]{0:T(512)S(1)} %bitcast.165, bf16[512]{0:T(512)(128)(2,1)S(1)} %reshape.348, bf16[]{:T(256)} %constant.126.clone.1), kind=kCustom, calls=%fused_computation.150 | custom fusion | bytes 1538 | tf_op jit(solution)/shard_map/scatter | solution.py:121
  119.3 30.4 %reduce-scatter.3.cloned.1.call-done = bf16[1,256,384]{2,1,0:T(8,128)(2,1)} async-done(((bf16[8,256,384]{2,1,0:T(8,128)(2,1)}), bf16[1,256,384]{2,1,0:T(8,128)(2,1)}) %reduce-scatter.3.cloned.1.call-update) | async-done | bytes 196624 | tf_op jit(solution)/shard_map/reduce_scatter | solution.py:94
  151.3 3.3 gather_fusion
  158.7 11.4 %all-to-all-start.1 = ((bf16[32,24,512]{2,1,0:T(8,128)(2,1)}), bf16[32,24,512]{2,1,0:T(8,128)(2,1)S(1)}, u32[]{:S(2)}, u32[]{:S(2)}) async-start(bf16[32,24,512]{2,1,0:T(8,128)(2,1)} %bitcast.15), calls=%async_computation.2 | async-start | bytes 1572864 | tf_op jit(solution)/shard_map/all_to_all | solution.py:124
  170.2 14.1 %all-to-all-done.1 = bf16[32,24,512]{2,1,0:T(8,128)(2,1)S(1)} async-done(((bf16[32,24,512]{2,1,0:T(8,128)(2,1)}), bf16[32,24,512]{2,1,0:T(8,128)(2,1)S(1)}, u32[]{:S(2)}, u32[]{:S(2)}) %all-to-all-start.1) | async-done | bytes 786464 | tf_op jit(solution)/shard_map/all_to_all | solution.py:124
  185.7 5.0 %copy.212 = bf16[80,8,8,384]{3,2,1,0:T(8,128)(2,1)} copy(bf16[80,8,8,384]{3,1,2,0:T(8,128)(2,1)} %bitcast.152) | data formatting | bytes 7864320
  190.7 50.0 %all-gather.3.cloned.1.call-done = bf16[6208,384]{1,0:T(8,128)(2,1)} async-done(((bf16[776,384]{1,0:T(8,128)(2,1)}), bf16[6208,384]{1,0:T(8,128)(2,1)}) %all-gather.3.cloned.1.call-update) | async-done | bytes 4767760 | tf_op jit(solution)/shard_map/all_gather | solution.py:132
  242.4 7.2 %fusion.76 = f32[768,640,1]{1,0,2:T(8,128)S(1)} fusion(bf16[8,384,640]{2,1,0:T(8,128)(2,1)} %bitcast.176, bf16[8,776,384]{2,1,0:T(8,128)(2,1)} %bitcast.173, f32[8,384]{1,0:T(8,128)S(1)} %bitcast.158, f32[768]{0:T(1024)S(1)} %add_rsqrt_fusion), kind=kOutput, calls=%fused_computation.159 | convolution fusion | flops 3029336064 | bytes 10632192 | tf_op jit(solution)/shard_map/grc,gcf->rf/dot_general | solution.py:152
  249.7 4.0 %fusion.9 = bf16[768,640,1]{1,0,2:T(8,128)(2,1)S(1)} fusion(bf16[8,384,640]{2,1,0:T(8,128)(2,1)S(1)} %bitcast.177, f32[768,640,1]{1,0,2:T(8,128)S(1)} %fusion.76, bf16[8,776,384]{2,1,0:T(8,128)(2,1)S(1)} %bitcast.175, f32[8,384]{1,0:T(8,128)S(1)} %bitcast.159, f32[768]{0:T(1024)S(1)} %add_rsqrt_fusion), kind=kOutput, calls=%fused_computation.18 | convolution fusion | flops 3032285184 | bytes 11616256 | tf_op jit(solution)/shard_map/grc,gcf->rf/dot_general | solution.py:158
  253.8 5.6 %convert_bitcast_fusion = bf16[8,768,384]{2,1,0:T(8,128)(2,1)} fusion(bf16[768,640,1]{1,0,2:T(8,128)(2,1)S(1)} %fusion.9, bf16[640,8,384]{2,1,0:T(8,128)(2,1)S(1)} %bitcast.153), kind=kOutput, calls=%fused_computation.5 | convolution fusion | flops 3022258176 | bytes 9633792 | tf_op jit(solution)/shard_map/rf,fgc->grc/dot_general | solution.py:166
  260.3 4.0 %select_reduce_fusion = (f32[768]{0:T(1024)S(1)}, f32[768]{0:T(1024)S(1)}) fusion(s32[768]{0:T(1024)S(1)} %convert_reduce_fusion, pred[32]{0:T(512)(128)(4,1)S(1)} %iota_compare_fusion.4, bf16[4,8,8,384]{3,2,1,0:T(8,128)(2,1)S(1)} %bitcast.178, bf16[8,776,384]{2,1,0:T(8,128)(2,1)} %bitcast.174, f32[8,384]{1,0:T(8,128)S(1)} %bitcast.160, ...), kind=kOutput, calls=%fused_computation.97 | convolution fusion | flops 160553472 | bytes 4939808 | tf_op jit(solution)/shard_map/grc,gce->re/dot_general | solution.py:143
  265.0 53.6 %reduce-scatter.5.cloned.1.call-done = bf16[1,768,384]{2,1,0:T(8,128)(2,1)} async-done(((bf16[8,768,384]{2,1,0:T(8,128)(2,1)}), bf16[1,768,384]{2,1,0:T(8,128)(2,1)}) %reduce-scatter.5.cloned.1.call-update) | async-done | bytes 589840 | tf_op jit(solution)/shard_map/reduce_scatter | solution.py:169
  320.7 7.6 %all-to-all-start.2 = ((bf16[32,24,512]{2,1,0:T(8,128)(2,1)}), bf16[32,24,512]{2,1,0:T(8,128)(2,1)S(1)}, u32[]{:S(2)}, u32[]{:S(2)}) async-start(bf16[32,24,512]{2,1,0:T(8,128)(2,1)} %maximum_maximum_fusion), calls=%async_computation.4 | async-start | bytes 1572864 | tf_op jit(solution)/shard_map/all_to_all | solution.py:174
  328.3 14.2 %all-to-all-done.2 = bf16[32,24,512]{2,1,0:T(8,128)(2,1)S(1)} async-done(((bf16[32,24,512]{2,1,0:T(8,128)(2,1)}), bf16[32,24,512]{2,1,0:T(8,128)(2,1)S(1)}, u32[]{:S(2)}, u32[]{:S(2)}) %all-to-all-start.2) | async-done | bytes 786464 | tf_op jit(solution)/shard_map/all_to_all | solution.py:174
  (162 shorter events, 49.8 us)
Async XLA Ops:
  6.5 41.2 %copy-start = (bf16[256,512]{1,0:T(8,128)(2,1)S(1)}, bf16[256,512]{1,0:T(8,128)(2,1)}, u32[]{:S(2)}) copy-start(bf16[256,512]{1,0:T(8,128)(2,1)} %param.17) | copy-start | bytes 786436
  6.5 19.5 %copy-start.13 = (bf16[96,512]{1,0:T(8,128)(2,1)S(1)}, bf16[96,512]{1,0:T(8,128)(2,1)}, u32[]{:S(2)}) copy-start(bf16[96,512]{1,0:T(8,128)(2,1)} %param.22) | copy-start | bytes 294916
  10.3 17.8 %copy-start.9 = (bf16[256,512]{0,1:T(8,128)(2,1)}, bf16[256,512]{0,1:T(8,128)(2,1)S(1)}, u32[]{:S(2)}) copy-start(bf16[256,512]{0,1:T(8,128)(2,1)S(1)} %copy.206) | copy-start | bytes 786436
  11.9 8.0 %collective-permute-start = (f32[4,136,128]{2,1,0:T(8,128)S(1)}, f32[4,136,128]{2,1,0:T(8,128)S(1)}, u32[]{:S(2)}, u32[]{:S(2)}) collective-permute-start(f32[4,136,128]{2,1,0:T(8,128)S(1)} %maximum_maximum_fusion.2), channel_id=1, source_target_pairs={{0,8},{8,16},{16,24},{24,32},{32,40},{40,48},{48,56},{56,64},{64,7... | collective-permute-start | bytes 835592 | tf_op jit(solution)/shard_map/ppermute | solution.py:30
  22.2 15.7 %collective-permute-start.1 = (f32[4,136,128]{2,1,0:T(8,128)}, f32[4,136,128]{2,1,0:T(8,128)}, u32[]{:S(2)}, u32[]{:S(2)}) collective-permute-start(f32[4,136,128]{2,1,0:T(8,128)} %maximum_maximum_fusion.3), channel_id=1, source_target_pairs={{0,16},{8,24},{16,32},{24,40},{32,48},{40,56},{48,64},{56,72},{64,... | collective-permute-start | bytes 835592 | tf_op jit(solution)/shard_map/ppermute | solution.py:30
  28.0 78.3 %all-to-all-start = ((bf16[32,96,512]{2,1,0:T(8,128)(2,1)}), bf16[32,96,512]{2,1,0:T(8,128)(2,1)S(1)}, u32[]{:S(2)}, u32[]{:S(2)}) async-start(bf16[32,96,512]{2,1,0:T(8,128)(2,1)} %stack.2), calls=%async_computation | async-start | bytes 6291456 | tf_op jit(solution)/shard_map/all_to_all | solution.py:89
  37.6 51.4 %copy-start.15 = (bf16[512]{0:T(512)(128)(2,1)S(1)}, bf16[512]{0:T(512)(128)(2,1)}, u32[]{:S(2)}) copy-start(bf16[512]{0:T(512)(128)(2,1)} %param.21) | copy-start | bytes 3076
  37.7 112.1 %reduce-scatter.3.cloned.1.call-start = ((), (), s32[]{:S(2)}) async-start(), calls=%async_computation.5 | async-start | bytes 1769472 | tf_op jit(solution)/shard_map/reduce_scatter | solution.py:94
  42.2 36.2 %collective-permute-start.2 = (f32[4,136,128]{2,1,0:T(8,128)}, f32[4,136,128]{2,1,0:T(8,128)}, u32[]{:S(2)}, u32[]{:S(2)}) collective-permute-start(f32[4,136,128]{2,1,0:T(8,128)} %maximum_maximum_fusion.4), channel_id=1, source_target_pairs={{0,32},{8,40},{16,48},{24,56},{32,64},{40,72},{48,80},{56,88},{64,... | collective-permute-start | bytes 835592 | tf_op jit(solution)/shard_map/ppermute | solution.py:30
  50.1 50.3 %copy-start.4 = (f32[4,136,128]{2,1,0:T(8,128)S(1)}, f32[4,136,128]{2,1,0:T(8,128)}, u32[]{:S(2)}) copy-start(f32[4,136,128]{2,1,0:T(8,128)} %copy-done.3) | copy-start | bytes 835588
  50.1 54.5 %copy-start.1 = (f32[4,136,128]{2,1,0:T(8,128)S(1)}, f32[4,136,128]{2,1,0:T(8,128)}, u32[]{:S(2)}) copy-start(f32[4,136,128]{2,1,0:T(8,128)} %constant.121.clone.1) | copy-start | bytes 835588
  50.1 54.5 %copy-start.8 = (f32[4,136,128]{2,1,0:T(8,128)S(1)}, f32[4,136,128]{2,1,0:T(8,128)}, u32[]{:S(2)}) copy-start(f32[4,136,128]{2,1,0:T(8,128)} %copy-done.7) | copy-start | bytes 835588
  50.1 54.5 %copy-start.12 = (f32[256,4,128]{0,2,1:T(8,128)S(1)}, f32[256,4,128]{0,2,1:T(8,128)}, u32[]{:S(2)}) copy-start(f32[256,4,128]{0,2,1:T(8,128)} %convolution_bitcast_fusion.1) | copy-start | bytes 1572868
  81.3 12.7 %collective-permute-start.3 = (f32[4,136,128]{2,1,0:T(8,128)S(1)}, f32[4,136,128]{2,1,0:T(8,128)S(1)}, u32[]{:S(2)}, u32[]{:S(2)}) collective-permute-start(f32[4,136,128]{2,1,0:T(8,128)S(1)} %maximum_maximum_fusion.5), channel_id=1, source_target_pairs={{0,64},{8,72},{16,80},{24,88},{32,96},{40,104},{48,112},{56,120},{... | collective-permute-start | bytes 835592 | tf_op jit(solution)/shard_map/ppermute | solution.py:30
  95.2 9.4 %collective-permute-start.4 = (f32[4,136,128]{2,1,0:T(8,128)S(1)}, f32[4,136,128]{2,1,0:T(8,128)S(1)}, u32[]{:S(2)}, u32[]{:S(2)}) collective-permute-start(f32[4,136,128]{2,1,0:T(8,128)S(1)} %maximum_maximum_fusion.6), channel_id=1, source_target_pairs={{0,128},{8,136},{16,144},{24,152},{32,160},{40,168},{48,176},{56,1... | collective-permute-start | bytes 835592 | tf_op jit(solution)/shard_map/ppermute | solution.py:30
  151.3 18.8 %copy-start.16 = (bf16[384]{0:T(512)(128)(2,1)S(1)}, bf16[384]{0:T(512)(128)(2,1)}, u32[]{:S(2)}) copy-start(bf16[384]{0:T(512)(128)(2,1)} %param.24) | copy-start | bytes 2308
  158.7 25.6 %all-to-all-start.1 = ((bf16[32,24,512]{2,1,0:T(8,128)(2,1)}), bf16[32,24,512]{2,1,0:T(8,128)(2,1)S(1)}, u32[]{:S(2)}, u32[]{:S(2)}) async-start(bf16[32,24,512]{2,1,0:T(8,128)(2,1)} %bitcast.15), calls=%async_computation.2 | async-start | bytes 1572864 | tf_op jit(solution)/shard_map/all_to_all | solution.py:124
  170.1 70.7 %all-gather.3.cloned.1.call-start = ((), (), s32[]{:S(2)}) async-start(), calls=%async_computation.7 | async-start | bytes 5363712 | tf_op jit(solution)/shard_map/all_gather | solution.py:132
  185.7 132.9 %reduce-scatter.5.cloned.1.call-start = ((), (), s32[]{:S(2)}) async-start(), calls=%async_computation.6 | async-start | bytes 5308416 | tf_op jit(solution)/shard_map/reduce_scatter | solution.py:169
  242.4 7.3 %copy-start.17 = (bf16[6208,384]{1,0:T(8,128)(2,1)S(1)}, bf16[6208,384]{1,0:T(8,128)(2,1)}, u32[]{:S(2)}) copy-start(bf16[6208,384]{1,0:T(8,128)(2,1)} %all-gather.3.cloned.1.call-done) | copy-start | bytes 14303236
  242.4 7.3 %copy-start.18 = (bf16[1,3072,640]{2,1,0:T(8,128)(2,1)S(1)}, bf16[1,3072,640]{2,1,0:T(8,128)(2,1)}, u32[]{:S(2)}) copy-start(bf16[1,3072,640]{2,1,0:T(8,128)(2,1)} %param.28) | copy-start | bytes 11796484
  320.7 21.8 %all-to-all-start.2 = ((bf16[32,24,512]{2,1,0:T(8,128)(2,1)}), bf16[32,24,512]{2,1,0:T(8,128)(2,1)S(1)}, u32[]{:S(2)}, u32[]{:S(2)}) async-start(bf16[32,24,512]{2,1,0:T(8,128)(2,1)} %maximum_maximum_fusion), calls=%async_computation.4 | async-start | bytes 1572864 | tf_op jit(solution)/shard_map/all_to_all | solution.py:174
  342.6 4.4 %copy-start.10 = (bf16[256,384]{1,0:T(8,128)(2,1)S(1)}, bf16[256,384]{1,0:T(8,128)(2,1)}, u32[]{:S(2)}) copy-start(bf16[256,384]{1,0:T(8,128)(2,1)} %param.23) | copy-start | bytes 589828
  342.6 4.4 %copy-start.11 = (bf16[1,256,384]{2,1,0:T(8,128)(2,1)S(1)}, bf16[1,256,384]{2,1,0:T(8,128)(2,1)}, u32[]{:S(2)}) copy-start(bf16[1,256,384]{2,1,0:T(8,128)(2,1)} %reduce-scatter.3.cloned.1.call-done) | copy-start | bytes 589828
  (7 other events, 14.5 us)
Sparse Core Ops, SparseCore 0:
  109.6 40.0 reduce-scatter.2
  185.8 54.9 all-gather.2
  259.5 58.9 reduce-scatter.4
